TPU v7x, 32 devices: a whole 2x2x4 slice. The times are simulated.
32 devices in a mesh: section: 4 (over z), dp: 8 (over y, x, core).
Axes of the slice: x: 2, y: 2, z: 4, core: 2. Of those that a mesh axis runs over, the one named last changes fastest.
Arguments:
- layer_inputs: bfloat16 [4, 8, 128, 2560], P('section', 'dp'), may hold values from -6 to 6
- w_bc: bfloat16 [4, 2560, 256], P('section'), may hold values from -0.125 to 0.125
- log_decay: float32 [4, 8, 128, 40], P('section', 'dp'), may hold values from -1.7 to 0, as said below
- top_grad: bfloat16 [8, 128, 2560], P('dp'), may hold values from -6 to 6
Outputs:
- grad_inputs: bfloat16 [4, 8, 128, 2560], P('section', 'dp')
- grad_w: float32 [4, 2560, 256], P('section', 'dp')
Inputs may be any that keep to these rules, and one draw needn't show every extreme that they name: `log_decay`: every entry is negative.
All inputs are finite; a program needn't handle non-finite values.
Results may differ from a plain program's by a relative error of at most 0.0085.
Values may be sent and summed in bfloat16 or wider, within the bound.
No kernel may reach another device: no remote copies, remote signals or barrier semaphores. Data moves between devices by JAX's collectives and lax.ppermute only.
A program may use at most 64 MiB of HBM per device.

v0:
```python
import jax
import jax.numpy as jnp
from jax import lax
from jax.sharding import PartitionSpec as P

MICRO = 4


def shortened(value):
    return jax.tree.map(lambda a: a.astype(jnp.bfloat16) if a.dtype == jnp.float32 else a, value)


def passed_along(block, axis, distance):
    devices = range(lax.axis_size(axis))
    route = [(i - distance, i) for i in devices if i - distance in devices]
    return lax.ppermute(block, axis, route)


def block_terms(inputs_b, in_b, out_b, rates, grads_b, carried, state_in, factor):
    length = inputs_b.shape[0]
    cumulative = jnp.cumsum(rates, axis=0)
    ending = cumulative[-1]
    locations = jnp.arange(length)
    lower_mask = (locations[:, None] >= locations[None, :])[:, :, None]
    spread = jnp.where(lower_mask, cumulative[:, None, :] - cumulative[None, :, :], 0.0)
    decays = jnp.where(lower_mask, jnp.exp(spread), 0.0)
    tail_decay = jnp.exp(ending[None, :] - cumulative)
    leading = jnp.exp(cumulative)
    scores = jnp.dot(out_b, in_b.T, preferred_element_type=jnp.float32)
    weighted = (factor * decays * scores[:, :, None]).astype(jnp.bfloat16)
    carried_b = carried.astype(jnp.bfloat16)
    state_b = state_in.astype(jnp.bfloat16)
    grad_feats = jnp.einsum("kjh,khp->jhp", weighted, grads_b, preferred_element_type=jnp.float32)
    grad_feats = grad_feats + tail_decay[:, :, None] * jnp.einsum(
        "hpn,jn->jhp", carried_b, in_b, preferred_element_type=jnp.float32
    )
    pair_dots = jnp.einsum("khp,jhp->kjh", grads_b, inputs_b, preferred_element_type=jnp.float32)
    mixing = jnp.sum(decays * pair_dots, axis=2).astype(jnp.bfloat16)
    tail_inputs = (tail_decay[:, :, None] * inputs_b.astype(jnp.float32)).astype(jnp.bfloat16)
    lead_grads = (leading[:, :, None] * grads_b.astype(jnp.float32)).astype(jnp.bfloat16)
    grad_inmap = factor * jnp.dot(mixing.T, out_b, preferred_element_type=jnp.float32)
    grad_inmap = grad_inmap + jnp.einsum(
        "jhp,hpn->jn", tail_inputs, carried_b, preferred_element_type=jnp.float32
    )
    grad_outmap = factor * (
        jnp.dot(mixing, in_b, preferred_element_type=jnp.float32)
        + jnp.einsum("ihp,hpn->in", lead_grads, state_b, preferred_element_type=jnp.float32)
    )
    carry_out = factor * jnp.einsum(
        "khp,kn->hpn", lead_grads, out_b, preferred_element_type=jnp.float32
    )
    carry_out = carry_out + jnp.exp(ending)[:, None, None] * carried
    return (grad_feats, grad_inmap, grad_outmap, carry_out)


def block_end(inputs_b, in_b, rates, state_in):
    cumulative = jnp.cumsum(rates, axis=0)
    ending = cumulative[-1]
    tail_decay = jnp.exp(ending[None, :] - cumulative)
    tail_inputs = (tail_decay[:, :, None] * inputs_b.astype(jnp.float32)).astype(jnp.bfloat16)
    fresh = jnp.einsum("jhp,jn->hpn", tail_inputs, in_b, preferred_element_type=jnp.float32)
    return jnp.exp(ending)[:, None, None] * state_in + fresh


def split_block(inputs_c, map_block, head_count):
    length, features = inputs_c.shape
    state_size = map_block.shape[1] // 2
    inputs_b = inputs_c.reshape(length, head_count, features // head_count)
    in_b = map_block[:, :state_size]
    out_b = map_block[:, state_size:]
    return (inputs_b, in_b, out_b)


def block_back(inputs_c, map_block, rates, grads_c, carried, state_in, weights):
    length, features = inputs_c.shape
    head_count = rates.shape[1]
    factor = 0.25 / (map_block.shape[1] // 2)
    inputs_b, in_b, out_b = split_block(inputs_c, map_block, head_count)
    grads_b = grads_c.reshape(length, head_count, features // head_count)
    grad_feats, grad_inmap, grad_outmap, carry_out = block_terms(
        inputs_b, in_b, out_b, rates, grads_b, carried, state_in, factor
    )
    grad_bc = jnp.concatenate([grad_inmap, grad_outmap], axis=1).astype(jnp.bfloat16)
    back_proj = lax.dot_general(
        grad_bc, weights, (((1,), (1,)), ((), ())), preferred_element_type=jnp.float32
    )
    summed = grads_c.astype(jnp.float32) + grad_feats.reshape(length, features) + back_proj
    return (summed.astype(jnp.bfloat16), carry_out, grad_bc)


def layer_starts(inputs_s, bc_s, rates_s):
    head_count = rates_s.shape[1]
    features = inputs_s.shape[1]
    state_size = bc_s.shape[1] // 2
    block_len = inputs_s.shape[0] // MICRO
    state_now = jnp.zeros((head_count, features // head_count, state_size), jnp.float32)
    saved = []
    for block_no in range(MICRO):
        lo_row = block_no * block_len
        inputs_b, in_b, out_b = split_block(
            inputs_s[lo_row : lo_row + block_len], bc_s[lo_row : lo_row + block_len], head_count
        )
        saved.append(state_now)
        state_now = block_end(inputs_b, in_b, rates_s[lo_row : lo_row + block_len], state_now)
    return jnp.stack(saved)


def shards(layer_inputs, w_bc, log_decay, top_grad):
    sections = lax.axis_size("section")
    section_id = lax.axis_index("section")
    lay_dev, seq_dev, tok_len, features = layer_inputs.shape
    block_len = tok_len // MICRO
    bc_all = jnp.einsum(
        "lstd,ldc->lstc", layer_inputs, w_bc, preferred_element_type=jnp.float32
    ).astype(jnp.bfloat16)
    starts = jax.vmap(jax.vmap(layer_starts))(layer_inputs, bc_all, log_decay)
    is_top = section_id == sections - 1
    back_all = jax.vmap(block_back, in_axes=(0, 0, 0, 0, 0, 0, None))

    def advance(counter, loop_state):
        incoming, carried, grad_store, map_store = loop_state
        offset = counter - (sections - 1 - section_id)
        is_valid = (offset >= 0) & (offset < MICRO)
        block_no = jnp.clip(MICRO - 1 - offset, 0, MICRO - 1)
        row_start = block_no * block_len
        from_top = lax.dynamic_slice_in_dim(top_grad, row_start, block_len, 1)
        grad_block = jnp.where(is_top, from_top, incoming)

        def compute(stores):
            carried_in, grads_in, maps_in = stores
            current = grad_block
            for level_no in reversed(range(lay_dev)):
                inputs_c = lax.dynamic_slice_in_dim(layer_inputs[level_no], row_start, block_len, 1)
                map_block = lax.dynamic_slice_in_dim(bc_all[level_no], row_start, block_len, 1)
                rates = lax.dynamic_slice_in_dim(log_decay[level_no], row_start, block_len, 1)
                state_in = lax.dynamic_index_in_dim(starts[level_no], block_no, 1, keepdims=False)
                level_grads, carry_out, grad_bc = back_all(
                    inputs_c,
                    map_block,
                    rates,
                    current,
                    carried_in[level_no],
                    state_in,
                    w_bc[level_no],
                )
                carried_in = carried_in.at[level_no].set(carry_out)
                grads_in = grads_in.at[level_no].set(
                    lax.dynamic_update_slice_in_dim(grads_in[level_no], level_grads, row_start, 1)
                )
                maps_in = maps_in.at[level_no].set(
                    lax.dynamic_update_slice_in_dim(maps_in[level_no], grad_bc, row_start, 1)
                )
                current = level_grads
            return (current, (carried_in, grads_in, maps_in))

        def passing(stores):
            return (jnp.zeros_like(grad_block), stores)

        outgoing, updated = lax.cond(is_valid, compute, passing, (carried, grad_store, map_store))
        received = jax.tree.map(
            lambda part, own: part.astype(own.dtype),
            passed_along(shortened(outgoing), "section", -1),
            outgoing,
        )
        return (received, updated[0], updated[1], updated[2])

    initial = (
        jnp.zeros((seq_dev, block_len, features), jnp.bfloat16),
        jnp.zeros((lay_dev,) + starts.shape[1:2] + starts.shape[3:], jnp.float32),
        jnp.zeros(layer_inputs.shape, jnp.bfloat16),
        jnp.zeros(bc_all.shape, jnp.bfloat16),
    )
    final_state = lax.fori_loop(0, MICRO + sections - 1, advance, initial)
    grad_inputs = final_state[2]
    map_store = final_state[3]
    ways = lax.axis_size("dp")
    divisor = ways * seq_dev
    rows_here = layer_inputs.reshape(lay_dev, seq_dev * tok_len, features)
    rows_all = lax.all_to_all(rows_here, "dp", 2, 1, tiled=True)
    maps_here = map_store.reshape(lay_dev, seq_dev * tok_len, map_store.shape[-1])
    maps_all = lax.all_gather(maps_here, "dp", axis=1, tiled=True)
    grad_w = (
        jnp.einsum("lrd,lrc->ldc", rows_all, maps_all, preferred_element_type=jnp.float32) / divisor
    )
    return (grad_inputs, grad_w)


def solution(mesh):
    in_specs = (
        P("section", "dp", None, None),
        P("section", None, None),
        P("section", "dp", None, None),
        P("dp", None, None),
    )
    out_specs = (P("section", "dp", None, None), P("section", "dp", None))
    return jax.shard_map(shards, mesh=mesh, in_specs=in_specs, out_specs=out_specs, check_vma=False)
```

profile of v0, /device:TPU:0, one launch (start us, length us, event | category | flops | bytes accessed | tf_op | source)
XLA Modules:
  0.0 188.5 jit_solution(8316372705247162726)
XLA Ops:
  0.6 2.5 %copy.89 = bf16[1,128,2560]{1,0,2:T(2,128)(2,1)S(1)} copy(bf16[1,128,2560]{2,1,0:T(8,128)(2,1)} %bitcast.43) | data formatting | bytes 1310720 | tf_op jit(solution)/shard_map/reshape | solution.py:178
  3.7 14.3 %reduce.10 = bf16[2560,128]{1,0:T(8,128)(2,1)S(1)} reduce(bf16[2560,1,128]{2,1,0:T(2,128)(2,1)S(1)} %bitcast.178, bf16[]{:T(256)} %broadcast.353), dimensions={1}, to_apply=%bitcast.170.reduce_sub_computation | reduce | bytes 1310722
  17.9 1.0 reshape.676
  18.9 5.2 %all-to-all-start = ((bf16[8,2,20480]{2,1,0:T(2,128)(2,1)}), bf16[8,2,20480]{2,1,0:T(2,128)(2,1)}, u32[]{:S(2)}, u32[]{:S(2)}) async-start(bf16[8,2,20480]{2,1,0:T(2,128)(2,1)} %reshape.676), calls=%async_computation | async-start | bytes 1310720 | tf_op jit(solution)/shard_map/all_to_all | solution.py:179
  24.6 0.7 copy.88
  26.7 1.3 multiply_convert_fusion.3
  28.2 1.4 fusion.61
  31.3 1.9 %pad_maximum_fusion = bf16[1,1,4,40,64,128]{5,4,3,2,1,0:T(8,128)(2,1)} fusion(bf16[1,1,1,40,64,128]{5,4,3,2,1,0:T(8,128)(2,1)S(1)} %fusion.54, f32[1,1,1,40,64,128]{5,4,3,2,1,0:T(8,128)S(1)} %bitcast.177, f32[1,1,1,40,64,128]{5,4,3,2,1,0:T(8,128)S(1)} %bitcast.176, bf16[4]{0:T(256)(128)(2,1)S(1)} %pad.10.clone), kind=kLoop, calls=%fused_computation.78 | loop fusion | flops 3932160 | bytes 5898248 | tf_op jit(solution)/shard_map/vmap(vmap())/stack | solution.py:105
  33.4 0.9 broadcast_in_dim.49
  34.3 0.6 broadcast_in_dim.50
  34.9 139.4 %while.24 = (s32[]{:T(128)}, bf16[1,32,2560]{2,1,0:T(8,128)(2,1)S(1)}, f32[1,1,40,64,128]{4,3,2,1,0:T(8,128)S(1)}, bf16[1,1,128,2560]{3,2,1,0:T(8,128)(2,1)}, bf...) while((s32[]{:T(128)}, ...), condition=%wide.region_8.9_spmd, body=%wide.region_3.8_spmd.sunk | while | flops 140346368 | bytes 17553168 | solution.py:173
  35.0 1.3 collective-permute-start
  36.3 7.4 %collective-permute-done = bf16[1,32,2560]{2,1,0:T(8,128)(2,1)S(1)} collective-permute-done((bf16[1,32,2560]{2,1,0:T(8,128)(2,1)S(1)}, bf16[1,32,2560]{2,1,0:T(8,128)(2,1)S(1)}, u32[]{:S(2)}, u32[]{:S(2)}) %collective-permute-start) | collective-permute-done | bytes 163872 | tf_op jit(solution)/shard_map/while/body/eval_jaxpr/ppermute | solution.py:16
  43.7 1.3 collective-permute-start
  45.0 6.4 %collective-permute-done = bf16[1,32,2560]{2,1,0:T(8,128)(2,1)S(1)} collective-permute-done((bf16[1,32,2560]{2,1,0:T(8,128)(2,1)S(1)}, bf16[1,32,2560]{2,1,0:T(8,128)(2,1)S(1)}, u32[]{:S(2)}, u32[]{:S(2)}) %collective-permute-start) | collective-permute-done | bytes 163872 | tf_op jit(solution)/shard_map/while/body/eval_jaxpr/ppermute | solution.py:16
  51.4 1.3 collective-permute-start
  52.7 42.5 %collective-permute-done = bf16[1,32,2560]{2,1,0:T(8,128)(2,1)S(1)} collective-permute-done((bf16[1,32,2560]{2,1,0:T(8,128)(2,1)S(1)}, bf16[1,32,2560]{2,1,0:T(8,128)(2,1)S(1)}, u32[]{:S(2)}, u32[]{:S(2)}) %collective-permute-start) | collective-permute-done | bytes 163872 | tf_op jit(solution)/shard_map/while/body/eval_jaxpr/ppermute | solution.py:16
  95.2 12.6 %conditional.2 = (bf16[1,32,2560]{2,1,0:T(8,128)(2,1)S(1)}, f32[1,1,40,64,128]{4,3,2,1,0:T(8,128)S(1)}, bf16[1,1,128,2560]{3,2,1,0:T(8,128)(2,1)}, bf16[1,1,128,256]{3,2,1,0:T(8,128)(2,1)}) conditional(s32[]{:T(128)} %convert_element_type.236, (f32[1,1,40,64,128]{4,3,2,1,0:T(8,128)S(1)}, bf16[1,1,128,2560]{3,2,1,0:T(8,128)(2,1)}, ...), branch_computations={%region_4.4_spmd, %region_5.7_spmd} | conditional | flops 140346368 | bytes 16897460 | solution.py:159
  95.2 0.7 dynamic-slice_bitcast_fusion.1
  96.4 1.0 fusion.18
  98.1 1.0 multiply_convert_fusion.2
  100.6 1.4 fusion.13
  102.0 0.6 maximum_dynamic-update-slice_fusion
  102.7 0.7 fusion.5
  104.6 2.5 %bitcast_dynamic-update-slice_fusion = (bf16[1,1,128,2560]{3,2,1,0:T(8,128)(2,1)}, bf16[1,32,2560]{2,1,0:T(8,128)(2,1)S(1)}) fusion(bf16[1,1,128,2560]{3,2,1,0:T(8,128)(2,1)} %get-tuple-element.483, s32[]{:T(128)S(6)} %select_n.90, bf16[1,2560,256]{2,1,0:T(8,128)(2,1)} %get-tuple-element.482, bf16[32,128]{1,0:T(8,128)(2,1)S(1)} %fusion.13, ...), kind=kOutput, calls=%fused_computation.46 | convolution fusion | flops 42303488 | bytes 2146308 | tf_op jit(solution)/shard_map/while/body/eval_jaxpr/cond/branch_1_fun/vmap()/dot_general | solution.py:84
  107.1 0.7 fusion.3
  107.8 1.3 collective-permute-start
  109.1 5.9 %collective-permute-done = bf16[1,32,2560]{2,1,0:T(8,128)(2,1)S(1)} collective-permute-done((bf16[1,32,2560]{2,1,0:T(8,128)(2,1)S(1)}, bf16[1,32,2560]{2,1,0:T(8,128)(2,1)S(1)}, u32[]{:S(2)}, u32[]{:S(2)}) %collective-permute-start) | collective-permute-done | bytes 163872 | tf_op jit(solution)/shard_map/while/body/eval_jaxpr/ppermute | solution.py:16
  115.0 12.6 %conditional.2 = (bf16[1,32,2560]{2,1,0:T(8,128)(2,1)S(1)}, f32[1,1,40,64,128]{4,3,2,1,0:T(8,128)S(1)}, bf16[1,1,128,2560]{3,2,1,0:T(8,128)(2,1)}, bf16[1,1,128,256]{3,2,1,0:T(8,128)(2,1)}) conditional(s32[]{:T(128)} %convert_element_type.236, (f32[1,1,40,64,128]{4,3,2,1,0:T(8,128)S(1)}, bf16[1,1,128,2560]{3,2,1,0:T(8,128)(2,1)}, ...), branch_computations={%region_4.4_spmd, %region_5.7_spmd} | conditional | flops 140346368 | bytes 16897460 | solution.py:159
  115.0 0.7 dynamic-slice_bitcast_fusion.1
  116.2 1.0 fusion.18
  117.8 1.0 multiply_convert_fusion.2
  120.4 1.4 fusion.13
  121.8 0.6 maximum_dynamic-update-slice_fusion
  122.5 0.7 fusion.5
  124.4 2.5 %bitcast_dynamic-update-slice_fusion = (bf16[1,1,128,2560]{3,2,1,0:T(8,128)(2,1)}, bf16[1,32,2560]{2,1,0:T(8,128)(2,1)S(1)}) fusion(bf16[1,1,128,2560]{3,2,1,0:T(8,128)(2,1)} %get-tuple-element.483, s32[]{:T(128)S(6)} %select_n.90, bf16[1,2560,256]{2,1,0:T(8,128)(2,1)} %get-tuple-element.482, bf16[32,128]{1,0:T(8,128)(2,1)S(1)} %fusion.13, ...), kind=kOutput, calls=%fused_computation.46 | convolution fusion | flops 42303488 | bytes 2146308 | tf_op jit(solution)/shard_map/while/body/eval_jaxpr/cond/branch_1_fun/vmap()/dot_general | solution.py:84
  126.9 0.7 fusion.3
  127.6 1.3 collective-permute-start
  128.9 5.9 %collective-permute-done = bf16[1,32,2560]{2,1,0:T(8,128)(2,1)S(1)} collective-permute-done((bf16[1,32,2560]{2,1,0:T(8,128)(2,1)S(1)}, bf16[1,32,2560]{2,1,0:T(8,128)(2,1)S(1)}, u32[]{:S(2)}, u32[]{:S(2)}) %collective-permute-start) | collective-permute-done | bytes 163872 | tf_op jit(solution)/shard_map/while/body/eval_jaxpr/ppermute | solution.py:16
  134.8 12.6 %conditional.2 = (bf16[1,32,2560]{2,1,0:T(8,128)(2,1)S(1)}, f32[1,1,40,64,128]{4,3,2,1,0:T(8,128)S(1)}, bf16[1,1,128,2560]{3,2,1,0:T(8,128)(2,1)}, bf16[1,1,128,256]{3,2,1,0:T(8,128)(2,1)}) conditional(s32[]{:T(128)} %convert_element_type.236, (f32[1,1,40,64,128]{4,3,2,1,0:T(8,128)S(1)}, bf16[1,1,128,2560]{3,2,1,0:T(8,128)(2,1)}, ...), branch_computations={%region_4.4_spmd, %region_5.7_spmd} | conditional | flops 140346368 | bytes 16897460 | solution.py:159
  134.8 0.7 dynamic-slice_bitcast_fusion.1
  136.0 1.0 fusion.18
  137.6 1.0 multiply_convert_fusion.2
  140.2 1.4 fusion.13
  141.6 0.6 maximum_dynamic-update-slice_fusion
  142.3 0.7 fusion.5
  144.2 2.5 %bitcast_dynamic-update-slice_fusion = (bf16[1,1,128,2560]{3,2,1,0:T(8,128)(2,1)}, bf16[1,32,2560]{2,1,0:T(8,128)(2,1)S(1)}) fusion(bf16[1,1,128,2560]{3,2,1,0:T(8,128)(2,1)} %get-tuple-element.483, s32[]{:T(128)S(6)} %select_n.90, bf16[1,2560,256]{2,1,0:T(8,128)(2,1)} %get-tuple-element.482, bf16[32,128]{1,0:T(8,128)(2,1)S(1)} %fusion.13, ...), kind=kOutput, calls=%fused_computation.46 | convolution fusion | flops 42303488 | bytes 2146308 | tf_op jit(solution)/shard_map/while/body/eval_jaxpr/cond/branch_1_fun/vmap()/dot_general | solution.py:84
  146.7 0.7 fusion.3
  147.4 1.3 collective-permute-start
  148.7 5.9 %collective-permute-done = bf16[1,32,2560]{2,1,0:T(8,128)(2,1)S(1)} collective-permute-done((bf16[1,32,2560]{2,1,0:T(8,128)(2,1)S(1)}, bf16[1,32,2560]{2,1,0:T(8,128)(2,1)S(1)}, u32[]{:S(2)}, u32[]{:S(2)}) %collective-permute-start) | collective-permute-done | bytes 163872 | tf_op jit(solution)/shard_map/while/body/eval_jaxpr/ppermute | solution.py:16
  154.6 12.6 %conditional.2 = (bf16[1,32,2560]{2,1,0:T(8,128)(2,1)S(1)}, f32[1,1,40,64,128]{4,3,2,1,0:T(8,128)S(1)}, bf16[1,1,128,2560]{3,2,1,0:T(8,128)(2,1)}, bf16[1,1,128,256]{3,2,1,0:T(8,128)(2,1)}) conditional(s32[]{:T(128)} %convert_element_type.236, (f32[1,1,40,64,128]{4,3,2,1,0:T(8,128)S(1)}, bf16[1,1,128,2560]{3,2,1,0:T(8,128)(2,1)}, ...), branch_computations={%region_4.4_spmd, %region_5.7_spmd} | conditional | flops 140346368 | bytes 16897460 | solution.py:159
  154.6 0.7 dynamic-slice_bitcast_fusion.1
  155.8 1.0 fusion.18
  157.4 1.0 multiply_convert_fusion.2
  160.0 1.4 fusion.13
  161.4 0.6 maximum_dynamic-update-slice_fusion
  162.1 0.7 fusion.5
  164.0 2.5 %bitcast_dynamic-update-slice_fusion = (bf16[1,1,128,2560]{3,2,1,0:T(8,128)(2,1)}, bf16[1,32,2560]{2,1,0:T(8,128)(2,1)S(1)}) fusion(bf16[1,1,128,2560]{3,2,1,0:T(8,128)(2,1)} %get-tuple-element.483, s32[]{:T(128)S(6)} %select_n.90, bf16[1,2560,256]{2,1,0:T(8,128)(2,1)} %get-tuple-element.482, bf16[32,128]{1,0:T(8,128)(2,1)S(1)} %fusion.13, ...), kind=kOutput, calls=%fused_computation.46 | convolution fusion | flops 42303488 | bytes 2146308 | tf_op jit(solution)/shard_map/while/body/eval_jaxpr/cond/branch_1_fun/vmap()/dot_general | solution.py:84
  166.4 0.7 fusion.3
  167.2 1.3 collective-permute-start
  168.5 5.9 %collective-permute-done = bf16[1,32,2560]{2,1,0:T(8,128)(2,1)S(1)} collective-permute-done((bf16[1,32,2560]{2,1,0:T(8,128)(2,1)S(1)}, bf16[1,32,2560]{2,1,0:T(8,128)(2,1)S(1)}, u32[]{:S(2)}, u32[]{:S(2)}) %collective-permute-start) | collective-permute-done | bytes 163872 | tf_op jit(solution)/shard_map/while/body/eval_jaxpr/ppermute | solution.py:16
  174.4 10.2 %all-gather = bf16[1,1,1024,256]{3,2,1,0:T(8,128)(2,1)S(1)} all-gather(bf16[1,1,128,256]{3,2,1,0:T(8,128)(2,1)} %get-tuple-element.508), channel_id=2, replica_groups=mesh['section'=4,'dp'=8] {'dp'}, dimensions={2}, use_global_device_ids=true | all-gather | bytes 589824 | tf_op jit(solution)/shard_map/all_gather | solution.py:181
  184.6 2.3 %reshape.677 = bf16[2560,1,128]{2,1,0:T(2,128)(2,1)S(1)} reshape(bf16[8,2,20480]{2,1,0:T(2,128)(2,1)} %all-to-all-done) | data formatting | bytes 1310720
  187.5 1.1 fusion.57
  (145 shorter events, 20.6 us)
Async XLA Ops:
  17.9 6.2 %copy-start.1 = (f32[1,1,128,40]{2,3,1,0:T(8,128)S(1)}, f32[1,1,128,40]{2,3,1,0:T(8,128)}, u32[]{:S(2)}) copy-start(f32[1,1,128,40]{2,3,1,0:T(8,128)} %param.16) | copy-start | bytes 61444
  18.9 165.6 %all-to-all-start = ((bf16[8,2,20480]{2,1,0:T(2,128)(2,1)}), bf16[8,2,20480]{2,1,0:T(2,128)(2,1)}, u32[]{:S(2)}, u32[]{:S(2)}) async-start(bf16[8,2,20480]{2,1,0:T(2,128)(2,1)} %reshape.676), calls=%async_computation | async-start | bytes 1310720 | tf_op jit(solution)/shard_map/all_to_all | solution.py:179
  26.7 1.6 copy-start
  35.0 8.7 %collective-permute-start = (bf16[1,32,2560]{2,1,0:T(8,128)(2,1)S(1)}, bf16[1,32,2560]{2,1,0:T(8,128)(2,1)S(1)}, u32[]{:S(2)}, u32[]{:S(2)}) collective-permute-start(bf16[1,32,2560]{2,1,0:T(8,128)(2,1)S(1)} %get-tuple-element.684), channel_id=1, source_target_pairs={{8,0},{16,8},{24,16},{9,1},{17,9},{25,17},{10,2},{18,10},{26,18},{... | collective-permute-start | bytes 491528 | tf_op jit(solution)/shard_map/while/body/eval_jaxpr/ppermute | solution.py:16
  43.7 7.7 %collective-permute-start = (bf16[1,32,2560]{2,1,0:T(8,128)(2,1)S(1)}, bf16[1,32,2560]{2,1,0:T(8,128)(2,1)S(1)}, u32[]{:S(2)}, u32[]{:S(2)}) collective-permute-start(bf16[1,32,2560]{2,1,0:T(8,128)(2,1)S(1)} %get-tuple-element.684), channel_id=1, source_target_pairs={{8,0},{16,8},{24,16},{9,1},{17,9},{25,17},{10,2},{18,10},{26,18},{... | collective-permute-start | bytes 491528 | tf_op jit(solution)/shard_map/while/body/eval_jaxpr/ppermute | solution.py:16
  51.4 43.8 %collective-permute-start = (bf16[1,32,2560]{2,1,0:T(8,128)(2,1)S(1)}, bf16[1,32,2560]{2,1,0:T(8,128)(2,1)S(1)}, u32[]{:S(2)}, u32[]{:S(2)}) collective-permute-start(bf16[1,32,2560]{2,1,0:T(8,128)(2,1)S(1)} %get-tuple-element.684), channel_id=1, source_target_pairs={{8,0},{16,8},{24,16},{9,1},{17,9},{25,17},{10,2},{18,10},{26,18},{... | collective-permute-start | bytes 491528 | tf_op jit(solution)/shard_map/while/body/eval_jaxpr/ppermute | solution.py:16
  107.8 7.2 %collective-permute-start = (bf16[1,32,2560]{2,1,0:T(8,128)(2,1)S(1)}, bf16[1,32,2560]{2,1,0:T(8,128)(2,1)S(1)}, u32[]{:S(2)}, u32[]{:S(2)}) collective-permute-start(bf16[1,32,2560]{2,1,0:T(8,128)(2,1)S(1)} %get-tuple-element.684), channel_id=1, source_target_pairs={{8,0},{16,8},{24,16},{9,1},{17,9},{25,17},{10,2},{18,10},{26,18},{... | collective-permute-start | bytes 491528 | tf_op jit(solution)/shard_map/while/body/eval_jaxpr/ppermute | solution.py:16
  127.6 7.2 %collective-permute-start = (bf16[1,32,2560]{2,1,0:T(8,128)(2,1)S(1)}, bf16[1,32,2560]{2,1,0:T(8,128)(2,1)S(1)}, u32[]{:S(2)}, u32[]{:S(2)}) collective-permute-start(bf16[1,32,2560]{2,1,0:T(8,128)(2,1)S(1)} %get-tuple-element.684), channel_id=1, source_target_pairs={{8,0},{16,8},{24,16},{9,1},{17,9},{25,17},{10,2},{18,10},{26,18},{... | collective-permute-start | bytes 491528 | tf_op jit(solution)/shard_map/while/body/eval_jaxpr/ppermute | solution.py:16
  147.4 7.2 %collective-permute-start = (bf16[1,32,2560]{2,1,0:T(8,128)(2,1)S(1)}, bf16[1,32,2560]{2,1,0:T(8,128)(2,1)S(1)}, u32[]{:S(2)}, u32[]{:S(2)}) collective-permute-start(bf16[1,32,2560]{2,1,0:T(8,128)(2,1)S(1)} %get-tuple-element.684), channel_id=1, source_target_pairs={{8,0},{16,8},{24,16},{9,1},{17,9},{25,17},{10,2},{18,10},{26,18},{... | collective-permute-start | bytes 491528 | tf_op jit(solution)/shard_map/while/body/eval_jaxpr/ppermute | solution.py:16
  167.2 7.2 %collective-permute-start = (bf16[1,32,2560]{2,1,0:T(8,128)(2,1)S(1)}, bf16[1,32,2560]{2,1,0:T(8,128)(2,1)S(1)}, u32[]{:S(2)}, u32[]{:S(2)}) collective-permute-start(bf16[1,32,2560]{2,1,0:T(8,128)(2,1)S(1)} %get-tuple-element.684), channel_id=1, source_target_pairs={{8,0},{16,8},{24,16},{9,1},{17,9},{25,17},{10,2},{18,10},{26,18},{... | collective-permute-start | bytes 491528 | tf_op jit(solution)/shard_map/while/body/eval_jaxpr/ppermute | solution.py:16
where the time goes:
time: 190 us; the launch traced here: 189 us
  waiting for transfers between devices  79.9 us (42%)
  matrix products  30.2 us (16%)
  other arithmetic  28.2 us (15%)
  local copies, waits for them, and re-layouts  24.2 us (13%)
  starting transfers between devices  14.2 us (7%)
  blocking collectives  10.2 us (5%)
    ppermute x7, waiting for transfers between devices, passed_along(): return lax.ppermute(block, axis, route)  79.9 us
    unnamed x1, other arithmetic  14.3 us
    all_gather x1, blocking collectives, shards(): maps_all = lax.all_gather(maps_here, 'dp', axis=1, tiled=True)  10.2 us
    dot_general x4, matrix products, block_back(): lax.dot_general(grad_bc, weights, (((1,), (1,)), ((), ())), preferred_ele...  9.94 us
    ppermute x7, starting transfers between devices, passed_along(): return lax.ppermute(block, axis, route)  9.04 us
    dot_general x4, matrix products, block_terms(): jnp.einsum('ihp,hpn->in', lead_grads, state_b, preferred_element_type=jnp...  5.47 us
    all_to_all x1, starting transfers between devices, shards(): rows_all = lax.all_to_all(rows_here, 'dp', 2, 1, tiled=True)  5.17 us
    unnamed x8, local copies, waits for them, and re-layouts  4 us
  transfers between devices with their start and end apart: 8, of which 7 were waited for; matrix products, arithmetic and copies ran while one was open for 32% of the time, Pallas kernels for 0%

commit v1 on v0

--- a/solution.py
+++ b/solution.py
@@ -176,7 +176,10 @@
     ways = lax.axis_size("dp")
     divisor = ways * seq_dev
     rows_here = layer_inputs.reshape(lay_dev, seq_dev * tok_len, features)
-    rows_all = lax.all_to_all(rows_here, "dp", 2, 1, tiled=True)
+    rows_all = jnp.concatenate(
+        lax.all_to_all(jnp.stack(jnp.split(rows_here, lax.axis_size("dp"), axis=2)), "dp", 0, 0),
+        axis=1,
+    )
     maps_here = map_store.reshape(lay_dev, seq_dev * tok_len, map_store.shape[-1])
     maps_all = lax.all_gather(maps_here, "dp", axis=1, tiled=True)
     grad_w = (

time: 190 us -> 181 us (0.953)
  other arithmetic: 28.2 us -> 13.9 us
  local copies, waits for them, and re-layouts: 24.2 us -> 27.8 us
  waiting for transfers between devices: 79.9 us -> 82.4 us
    unnamed x1 -> x0, other arithmetic: 14.3 us -> none
    cond x0 -> x16, local copies, waits for them, and re-layouts: none -> 3.04 us
    reshape x1 -> x0, local copies, waits for them, and re-layouts: 2.51 us -> none  [shards(): rows_here = layer_inputs.reshape(lay_dev, seq_dev * tok_len, features)]
    ppermute x7, waiting for transfers between devices: 79.9 us -> 82.4 us  [passed_along(): return lax.ppermute(block, axis, route)]
    unnamed x8 -> x12, local copies, waits for them, and re-layouts: 4 us -> 5.94 us
  transfers between devices with their start and end apart: 8 -> 8, of which waited for: 7 -> 7; matrix products, arithmetic and copies ran while one was open for 32% -> 33% of each run, Pallas kernels for 0% -> 0%
where the time goes in v1:
time: 181 us; the launch traced here: 180 us
  waiting for transfers between devices  82.4 us (46%)
  matrix products  30.3 us (17%)
  local copies, waits for them, and re-layouts  27.8 us (15%)
  starting transfers between devices  14.2 us (8%)
  other arithmetic  13.9 us (8%)
  blocking collectives  9.7 us (5%)
    ppermute x7, waiting for transfers between devices, passed_along(): return lax.ppermute(block, axis, route)  82.4 us
    dot_general x4, matrix products, block_back(): lax.dot_general(grad_bc, weights, (((1,), (1,)), ((), ())), preferred_ele...  9.95 us
    all_gather x1, blocking collectives, shards(): maps_all = lax.all_gather(maps_here, 'dp', axis=1, tiled=True)  9.7 us
    ppermute x7, starting transfers between devices, passed_along(): return lax.ppermute(block, axis, route)  9 us
    unnamed x12, local copies, waits for them, and re-layouts  5.94 us
    dot_general x4, matrix products, block_terms(): jnp.einsum('ihp,hpn->in', lead_grads, state_b, preferred_element_type=jnp...  5.47 us
    all_to_all x1, starting transfers between devices, shards(): lax.all_to_all(jnp.stack(jnp.split(rows_here, lax.axis_size('dp'), axis=2...  5.17 us
    convert_element_type x4, other arithmetic, block_terms(): (leading[:, :, None] * grads_b.astype(jnp.float32)).astype(jnp.bfloat16)  3.93 us
  transfers between devices with their start and end apart: 8, of which 7 were waited for; matrix products, arithmetic and copies ran while one was open for 33% of the time, Pallas kernels for 0%

profile of v1, /device:TPU:0, one launch (start us, length us, event | category | flops | bytes accessed | tf_op | source)
XLA Modules:
  0.0 179.7 jit_solution(12314841943728325290)
XLA Ops:
  0.6 1.4 copy.86
  2.1 0.6 fusion.78
  2.7 0.6 fusion.77
  3.3 0.6 fusion.76
  4.0 0.6 fusion.75
  4.6 0.6 fusion.74
  5.9 0.6 fusion.72
  6.5 0.6 fusion.71
  7.1 5.2 %all-to-all-start = ((bf16[8,1,128,320]{2,3,1,0:T(8,128)(2,1)}), bf16[8,1,128,320]{2,3,1,0:T(8,128)(2,1)}, u32[]{:S(2)}, u32[]{:S(2)}) async-start(bf16[8,1,128,320]{2,3,1,0:T(8,128)(2,1)} %fusion.71), calls=%async_computation | async-start | bytes 1310720 | tf_op jit(solution)/shard_map/all_to_all | solution.py:180
  12.9 0.7 copy.85
  14.9 1.3 multiply_convert_fusion.3
  16.5 1.4 fusion.61
  19.5 1.9 %pad_maximum_fusion = bf16[1,1,4,40,64,128]{5,4,3,2,1,0:T(8,128)(2,1)} fusion(bf16[1,1,1,40,64,128]{5,4,3,2,1,0:T(8,128)(2,1)S(1)} %fusion.54, f32[1,1,1,40,64,128]{5,4,3,2,1,0:T(8,128)S(1)} %bitcast.202, f32[1,1,1,40,64,128]{5,4,3,2,1,0:T(8,128)S(1)} %bitcast.201, bf16[4]{0:T(256)(128)(2,1)S(1)} %pad.10.clone), kind=kLoop, calls=%fused_computation.78 | loop fusion | flops 3932160 | bytes 5898248 | tf_op jit(solution)/shard_map/vmap(vmap())/stack | solution.py:105
  21.6 0.9 broadcast_in_dim.49
  22.5 144.9 %while.24 = (s32[]{:T(128)}, bf16[1,32,2560]{2,1,0:T(8,128)(2,1)S(1)}, f32[1,1,40,64,128]{4,3,2,1,0:T(8,128)S(1)}, bf16[1,1,128,2560]{3,2,1,0:T(8,128)(2,1)}, bf...) while((s32[]{:T(128)}, ...), condition=%wide.region_8.9_spmd, body=%wide.region_3.8_spmd.sunk | while | flops 140346368 | bytes 18077512 | solution.py:173
  22.6 1.3 collective-permute-start
  23.9 7.4 %collective-permute-done = bf16[1,32,2560]{2,1,0:T(8,128)(2,1)S(1)} collective-permute-done((bf16[1,32,2560]{2,1,0:T(8,128)(2,1)S(1)}, bf16[1,32,2560]{2,1,0:T(8,128)(2,1)S(1)}, u32[]{:S(2)}, u32[]{:S(2)}) %collective-permute-start) | collective-permute-done | bytes 163872 | tf_op jit(solution)/shard_map/while/body/eval_jaxpr/ppermute | solution.py:16
  31.3 1.3 collective-permute-start
  32.6 6.5 %collective-permute-done = bf16[1,32,2560]{2,1,0:T(8,128)(2,1)S(1)} collective-permute-done((bf16[1,32,2560]{2,1,0:T(8,128)(2,1)S(1)}, bf16[1,32,2560]{2,1,0:T(8,128)(2,1)S(1)}, u32[]{:S(2)}, u32[]{:S(2)}) %collective-permute-start) | collective-permute-done | bytes 163872 | tf_op jit(solution)/shard_map/while/body/eval_jaxpr/ppermute | solution.py:16
  39.2 1.3 collective-permute-start
  40.5 44.9 %collective-permute-done = bf16[1,32,2560]{2,1,0:T(8,128)(2,1)S(1)} collective-permute-done((bf16[1,32,2560]{2,1,0:T(8,128)(2,1)S(1)}, bf16[1,32,2560]{2,1,0:T(8,128)(2,1)S(1)}, u32[]{:S(2)}, u32[]{:S(2)}) %collective-permute-start) | collective-permute-done | bytes 163872 | tf_op jit(solution)/shard_map/while/body/eval_jaxpr/ppermute | solution.py:16
  85.3 13.3 %conditional.2 = (bf16[1,32,2560]{2,1,0:T(8,128)(2,1)S(1)}, f32[1,1,40,64,128]{4,3,2,1,0:T(8,128)S(1)}, bf16[1,1,128,2560]{3,2,1,0:T(8,128)(2,1)}, bf16[1,1,128,256]{3,2,1,0:T(8,128)(2,1)S(1)}) conditional(s32[]{:T(128)} %convert_element_type.236, (f32[1,1,40,64,128]{4,3,2,1,0:T(8,128)S(1)}, bf16[1,1,128,2560]{3,2,1,0:T(8,128)(2,1)}, ...), branch_computations={%region_4.4_spmd, %region_5.7_spmd} | conditional | flops 140346368 | bytes 17421804 | solution.py:159
  85.9 0.7 dynamic-slice_bitcast_fusion.1
  87.2 1.0 fusion.18
  88.8 1.0 multiply_convert_fusion.2
  91.4 1.4 fusion.13
  93.4 0.7 fusion.5
  95.3 2.5 %bitcast_dynamic-update-slice_fusion = (bf16[1,1,128,2560]{3,2,1,0:T(8,128)(2,1)}, bf16[1,32,2560]{2,1,0:T(8,128)(2,1)S(1)}) fusion(bf16[1,1,128,2560]{3,2,1,0:T(8,128)(2,1)} %get-tuple-element.483, s32[]{:T(128)S(6)} %select_n.90, bf16[1,2560,256]{2,1,0:T(8,128)(2,1)} %get-tuple-element.482, bf16[32,128]{1,0:T(8,128)(2,1)S(1)} %fusion.13, ...), kind=kOutput, calls=%fused_computation.46 | convolution fusion | flops 42303488 | bytes 2146308 | tf_op jit(solution)/shard_map/while/body/eval_jaxpr/cond/branch_1_fun/vmap()/dot_general | solution.py:84
  97.8 0.7 fusion.3
  98.7 1.3 collective-permute-start
  99.9 5.9 %collective-permute-done = bf16[1,32,2560]{2,1,0:T(8,128)(2,1)S(1)} collective-permute-done((bf16[1,32,2560]{2,1,0:T(8,128)(2,1)S(1)}, bf16[1,32,2560]{2,1,0:T(8,128)(2,1)S(1)}, u32[]{:S(2)}, u32[]{:S(2)}) %collective-permute-start) | collective-permute-done | bytes 163872 | tf_op jit(solution)/shard_map/while/body/eval_jaxpr/ppermute | solution.py:16
  105.9 13.3 %conditional.2 = (bf16[1,32,2560]{2,1,0:T(8,128)(2,1)S(1)}, f32[1,1,40,64,128]{4,3,2,1,0:T(8,128)S(1)}, bf16[1,1,128,2560]{3,2,1,0:T(8,128)(2,1)}, bf16[1,1,128,256]{3,2,1,0:T(8,128)(2,1)S(1)}) conditional(s32[]{:T(128)} %convert_element_type.236, (f32[1,1,40,64,128]{4,3,2,1,0:T(8,128)S(1)}, bf16[1,1,128,2560]{3,2,1,0:T(8,128)(2,1)}, ...), branch_computations={%region_4.4_spmd, %region_5.7_spmd} | conditional | flops 140346368 | bytes 17421804 | solution.py:159
  106.5 0.7 dynamic-slice_bitcast_fusion.1
  107.7 1.0 fusion.18
  109.3 1.0 multiply_convert_fusion.2
  111.9 1.4 fusion.13
  114.0 0.7 fusion.5
  115.8 2.5 %bitcast_dynamic-update-slice_fusion = (bf16[1,1,128,2560]{3,2,1,0:T(8,128)(2,1)}, bf16[1,32,2560]{2,1,0:T(8,128)(2,1)S(1)}) fusion(bf16[1,1,128,2560]{3,2,1,0:T(8,128)(2,1)} %get-tuple-element.483, s32[]{:T(128)S(6)} %select_n.90, bf16[1,2560,256]{2,1,0:T(8,128)(2,1)} %get-tuple-element.482, bf16[32,128]{1,0:T(8,128)(2,1)S(1)} %fusion.13, ...), kind=kOutput, calls=%fused_computation.46 | convolution fusion | flops 42303488 | bytes 2146308 | tf_op jit(solution)/shard_map/while/body/eval_jaxpr/cond/branch_1_fun/vmap()/dot_general | solution.py:84
  118.3 0.7 fusion.3
  119.2 1.3 collective-permute-start
  120.5 5.9 %collective-permute-done = bf16[1,32,2560]{2,1,0:T(8,128)(2,1)S(1)} collective-permute-done((bf16[1,32,2560]{2,1,0:T(8,128)(2,1)S(1)}, bf16[1,32,2560]{2,1,0:T(8,128)(2,1)S(1)}, u32[]{:S(2)}, u32[]{:S(2)}) %collective-permute-start) | collective-permute-done | bytes 163872 | tf_op jit(solution)/shard_map/while/body/eval_jaxpr/ppermute | solution.py:16
  126.4 13.3 %conditional.2 = (bf16[1,32,2560]{2,1,0:T(8,128)(2,1)S(1)}, f32[1,1,40,64,128]{4,3,2,1,0:T(8,128)S(1)}, bf16[1,1,128,2560]{3,2,1,0:T(8,128)(2,1)}, bf16[1,1,128,256]{3,2,1,0:T(8,128)(2,1)S(1)}) conditional(s32[]{:T(128)} %convert_element_type.236, (f32[1,1,40,64,128]{4,3,2,1,0:T(8,128)S(1)}, bf16[1,1,128,2560]{3,2,1,0:T(8,128)(2,1)}, ...), branch_computations={%region_4.4_spmd, %region_5.7_spmd} | conditional | flops 140346368 | bytes 17421804 | solution.py:159
  127.0 0.7 dynamic-slice_bitcast_fusion.1
  128.2 1.0 fusion.18
  129.9 1.0 multiply_convert_fusion.2
  132.4 1.4 fusion.13
  134.5 0.7 fusion.5
  136.4 2.5 %bitcast_dynamic-update-slice_fusion = (bf16[1,1,128,2560]{3,2,1,0:T(8,128)(2,1)}, bf16[1,32,2560]{2,1,0:T(8,128)(2,1)S(1)}) fusion(bf16[1,1,128,2560]{3,2,1,0:T(8,128)(2,1)} %get-tuple-element.483, s32[]{:T(128)S(6)} %select_n.90, bf16[1,2560,256]{2,1,0:T(8,128)(2,1)} %get-tuple-element.482, bf16[32,128]{1,0:T(8,128)(2,1)S(1)} %fusion.13, ...), kind=kOutput, calls=%fused_computation.46 | convolution fusion | flops 42303488 | bytes 2146308 | tf_op jit(solution)/shard_map/while/body/eval_jaxpr/cond/branch_1_fun/vmap()/dot_general | solution.py:84
  138.9 0.7 fusion.3
  139.7 1.3 collective-permute-start
  141.0 5.9 %collective-permute-done = bf16[1,32,2560]{2,1,0:T(8,128)(2,1)S(1)} collective-permute-done((bf16[1,32,2560]{2,1,0:T(8,128)(2,1)S(1)}, bf16[1,32,2560]{2,1,0:T(8,128)(2,1)S(1)}, u32[]{:S(2)}, u32[]{:S(2)}) %collective-permute-start) | collective-permute-done | bytes 163872 | tf_op jit(solution)/shard_map/while/body/eval_jaxpr/ppermute | solution.py:16
  146.9 13.3 %conditional.2 = (bf16[1,32,2560]{2,1,0:T(8,128)(2,1)S(1)}, f32[1,1,40,64,128]{4,3,2,1,0:T(8,128)S(1)}, bf16[1,1,128,2560]{3,2,1,0:T(8,128)(2,1)}, bf16[1,1,128,256]{3,2,1,0:T(8,128)(2,1)S(1)}) conditional(s32[]{:T(128)} %convert_element_type.236, (f32[1,1,40,64,128]{4,3,2,1,0:T(8,128)S(1)}, bf16[1,1,128,2560]{3,2,1,0:T(8,128)(2,1)}, ...), branch_computations={%region_4.4_spmd, %region_5.7_spmd} | conditional | flops 140346368 | bytes 17421804 | solution.py:159
  147.5 0.7 dynamic-slice_bitcast_fusion.1
  148.8 1.0 fusion.18
  150.4 1.0 multiply_convert_fusion.2
  153.0 1.4 fusion.13
  155.0 0.7 fusion.5
  156.9 2.5 %bitcast_dynamic-update-slice_fusion = (bf16[1,1,128,2560]{3,2,1,0:T(8,128)(2,1)}, bf16[1,32,2560]{2,1,0:T(8,128)(2,1)S(1)}) fusion(bf16[1,1,128,2560]{3,2,1,0:T(8,128)(2,1)} %get-tuple-element.483, s32[]{:T(128)S(6)} %select_n.90, bf16[1,2560,256]{2,1,0:T(8,128)(2,1)} %get-tuple-element.482, bf16[32,128]{1,0:T(8,128)(2,1)S(1)} %fusion.13, ...), kind=kOutput, calls=%fused_computation.46 | convolution fusion | flops 42303488 | bytes 2146308 | tf_op jit(solution)/shard_map/while/body/eval_jaxpr/cond/branch_1_fun/vmap()/dot_general | solution.py:84
  159.4 0.7 fusion.3
  160.2 1.3 collective-permute-start
  161.5 5.9 %collective-permute-done = bf16[1,32,2560]{2,1,0:T(8,128)(2,1)S(1)} collective-permute-done((bf16[1,32,2560]{2,1,0:T(8,128)(2,1)S(1)}, bf16[1,32,2560]{2,1,0:T(8,128)(2,1)S(1)}, u32[]{:S(2)}, u32[]{:S(2)}) %collective-permute-start) | collective-permute-done | bytes 163872 | tf_op jit(solution)/shard_map/while/body/eval_jaxpr/ppermute | solution.py:16
  167.4 9.7 %all-gather = bf16[1,1,1024,256]{3,2,1,0:T(8,128)(2,1)S(1)} all-gather(bf16[1,1,128,256]{3,2,1,0:T(8,128)(2,1)S(1)} %get-tuple-element.508), channel_id=2, replica_groups=mesh['section'=4,'dp'=8] {'dp'}, dimensions={2}, use_global_device_ids=true | all-gather | bytes 589824 | tf_op jit(solution)/shard_map/all_gather | solution.py:184
  177.1 1.5 copy.87
  178.7 1.1 fusion.57
  (164 shorter events, 25.7 us)
Async XLA Ops:
  2.0 10.3 %copy-start.1 = (f32[1,1,128,40]{2,3,1,0:T(8,128)S(1)}, f32[1,1,128,40]{2,3,1,0:T(8,128)}, u32[]{:S(2)}) copy-start(f32[1,1,128,40]{2,3,1,0:T(8,128)} %param.16) | copy-start | bytes 61444
  7.1 170.0 %all-to-all-start = ((bf16[8,1,128,320]{2,3,1,0:T(8,128)(2,1)}), bf16[8,1,128,320]{2,3,1,0:T(8,128)(2,1)}, u32[]{:S(2)}, u32[]{:S(2)}) async-start(bf16[8,1,128,320]{2,3,1,0:T(8,128)(2,1)} %fusion.71), calls=%async_computation | async-start | bytes 1310720 | tf_op jit(solution)/shard_map/all_to_all | solution.py:180
  14.9 1.6 copy-start
  22.6 8.7 %collective-permute-start = (bf16[1,32,2560]{2,1,0:T(8,128)(2,1)S(1)}, bf16[1,32,2560]{2,1,0:T(8,128)(2,1)S(1)}, u32[]{:S(2)}, u32[]{:S(2)}) collective-permute-start(bf16[1,32,2560]{2,1,0:T(8,128)(2,1)S(1)} %get-tuple-element.684), channel_id=1, source_target_pairs={{8,0},{16,8},{24,16},{9,1},{17,9},{25,17},{10,2},{18,10},{26,18},{... | collective-permute-start | bytes 491528 | tf_op jit(solution)/shard_map/while/body/eval_jaxpr/ppermute | solution.py:16
  31.3 7.8 %collective-permute-start = (bf16[1,32,2560]{2,1,0:T(8,128)(2,1)S(1)}, bf16[1,32,2560]{2,1,0:T(8,128)(2,1)S(1)}, u32[]{:S(2)}, u32[]{:S(2)}) collective-permute-start(bf16[1,32,2560]{2,1,0:T(8,128)(2,1)S(1)} %get-tuple-element.684), channel_id=1, source_target_pairs={{8,0},{16,8},{24,16},{9,1},{17,9},{25,17},{10,2},{18,10},{26,18},{... | collective-permute-start | bytes 491528 | tf_op jit(solution)/shard_map/while/body/eval_jaxpr/ppermute | solution.py:16
  39.2 46.2 %collective-permute-start = (bf16[1,32,2560]{2,1,0:T(8,128)(2,1)S(1)}, bf16[1,32,2560]{2,1,0:T(8,128)(2,1)S(1)}, u32[]{:S(2)}, u32[]{:S(2)}) collective-permute-start(bf16[1,32,2560]{2,1,0:T(8,128)(2,1)S(1)} %get-tuple-element.684), channel_id=1, source_target_pairs={{8,0},{16,8},{24,16},{9,1},{17,9},{25,17},{10,2},{18,10},{26,18},{... | collective-permute-start | bytes 491528 | tf_op jit(solution)/shard_map/while/body/eval_jaxpr/ppermute | solution.py:16
  85.3 0.6 copy-start.2
  97.8 0.8 copy-start.3
  98.7 7.2 %collective-permute-start = (bf16[1,32,2560]{2,1,0:T(8,128)(2,1)S(1)}, bf16[1,32,2560]{2,1,0:T(8,128)(2,1)S(1)}, u32[]{:S(2)}, u32[]{:S(2)}) collective-permute-start(bf16[1,32,2560]{2,1,0:T(8,128)(2,1)S(1)} %get-tuple-element.684), channel_id=1, source_target_pairs={{8,0},{16,8},{24,16},{9,1},{17,9},{25,17},{10,2},{18,10},{26,18},{... | collective-permute-start | bytes 491528 | tf_op jit(solution)/shard_map/while/body/eval_jaxpr/ppermute | solution.py:16
  105.9 0.6 copy-start.2
  118.3 0.8 copy-start.3
  119.2 7.2 %collective-permute-start = (bf16[1,32,2560]{2,1,0:T(8,128)(2,1)S(1)}, bf16[1,32,2560]{2,1,0:T(8,128)(2,1)S(1)}, u32[]{:S(2)}, u32[]{:S(2)}) collective-permute-start(bf16[1,32,2560]{2,1,0:T(8,128)(2,1)S(1)} %get-tuple-element.684), channel_id=1, source_target_pairs={{8,0},{16,8},{24,16},{9,1},{17,9},{25,17},{10,2},{18,10},{26,18},{... | collective-permute-start | bytes 491528 | tf_op jit(solution)/shard_map/while/body/eval_jaxpr/ppermute | solution.py:16
  126.4 0.6 copy-start.2
  138.9 0.8 copy-start.3
  139.7 7.2 %collective-permute-start = (bf16[1,32,2560]{2,1,0:T(8,128)(2,1)S(1)}, bf16[1,32,2560]{2,1,0:T(8,128)(2,1)S(1)}, u32[]{:S(2)}, u32[]{:S(2)}) collective-permute-start(bf16[1,32,2560]{2,1,0:T(8,128)(2,1)S(1)} %get-tuple-element.684), channel_id=1, source_target_pairs={{8,0},{16,8},{24,16},{9,1},{17,9},{25,17},{10,2},{18,10},{26,18},{... | collective-permute-start | bytes 491528 | tf_op jit(solution)/shard_map/while/body/eval_jaxpr/ppermute | solution.py:16
  146.9 0.6 copy-start.2
  159.4 0.8 copy-start.3
  160.2 7.2 %collective-permute-start = (bf16[1,32,2560]{2,1,0:T(8,128)(2,1)S(1)}, bf16[1,32,2560]{2,1,0:T(8,128)(2,1)S(1)}, u32[]{:S(2)}, u32[]{:S(2)}) collective-permute-start(bf16[1,32,2560]{2,1,0:T(8,128)(2,1)S(1)} %get-tuple-element.684), channel_id=1, source_target_pairs={{8,0},{16,8},{24,16},{9,1},{17,9},{25,17},{10,2},{18,10},{26,18},{... | collective-permute-start | bytes 491528 | tf_op jit(solution)/shard_map/while/body/eval_jaxpr/ppermute | solution.py:16
